TPU v7x, 32 devices: a whole 2x2x4 slice. The times are simulated.
32 devices in a mesh: dp: 2 (over y), row: 4 (over x, core), col: 4 (over z).
Axes of the slice: x: 2, y: 2, z: 4, core: 2. Of those that a mesh axis runs over, the one named last changes fastest.
Arguments:
- patches: bfloat16 [2, 512, 1456], P('dp', 'col', 'row'), may hold values from -6 to 6
- queries: bfloat16 [2, 512, 6144], P('dp', 'col', 'row'), may hold values from -6 to 6
- attn_keys: bfloat16 [2, 512, 6144], P('dp', 'col', 'row'), may hold values from -6 to 6
- attn_values: bfloat16 [2, 512, 6144], P('dp', 'col', 'row'), may hold values from -6 to 6
- out_weight: bfloat16 [6144, 12288], P('row', 'col'), may hold values from -0.15625 to 0.15625
- output_grad: bfloat16 [2, 512, 12288], P('dp', 'row', 'col'), may hold values from -4 to 4
Outputs:
- query_grad: float32 [2, 512, 6144], P('dp', 'col', 'row')
- key_grad: float32 [2, 512, 6144], P('dp', 'col', 'row')
- value_grad: float32 [2, 512, 6144], P('dp', 'col', 'row')
- out_weight_grad: float32 [6144, 12288], P('row', 'col')
- embed_weight_grad: float32 [1456, 12288], P('row', 'col')
All inputs are finite; a program needn't handle non-finite values.
Results may differ from a plain program's by a relative error of at most 0.025.
Values may be sent and summed in bfloat16 or wider, within the bound.
No kernel may reach another device: no remote copies, remote signals or barrier semaphores. Data moves between devices by JAX's collectives and lax.ppermute only.
A program may use at most 128 MiB of HBM per device.

v0:
```python
import jax
import jax.numpy as jnp
from jax import lax
from jax.sharding import PartitionSpec as P

DH = 128


def contract_rows(left, right):
    return lax.dot_general(
        left, right, (((0,), (0,)), ((), ())), preferred_element_type=jnp.float32
    )


def swap_dp(x):
    return lax.ppermute(x, "dp", [(0, 1), (1, 0)])


def body(patches, queries, attn_keys, attn_values, out_weight, output_grad):
    factor = DH ** (-0.5)
    local_rows = queries.shape[1]
    feature_width = queries.shape[2]
    head_count = feature_width // DH
    grad_other = swap_dp(output_grad)
    patch_other = swap_dp(lax.all_gather(patches, "col", axis=1, tiled=True))
    every_key, every_value, every_patch = (
        lax.all_gather(attn_keys, "col", axis=1, tiled=True),
        lax.all_gather(attn_values, "col", axis=1, tiled=True),
        lax.all_gather(patches, "col", axis=1, tiled=True),
    )
    local_query = queries[0].reshape(local_rows, head_count, DH)
    all_keys = every_key[0].reshape(-1, head_count, DH)
    all_values = every_value[0].reshape(-1, head_count, DH)
    scores = (
        jnp.einsum("qhd,khd->hqk", local_query, all_keys, preferred_element_type=jnp.float32)
        * factor
    )
    row_max = jnp.max(scores, axis=2, keepdims=True)
    log_total = row_max + jnp.log(jnp.sum(jnp.exp(scores - row_max), axis=2, keepdims=True))
    attn_probs = jnp.exp(scores - log_total).astype(jnp.bfloat16)
    attn_out = jnp.einsum(
        "hqk,khd->qhd", attn_probs, all_values, preferred_element_type=jnp.float32
    ).astype(jnp.bfloat16)
    out_local = attn_out.reshape(1, local_rows, feature_width)
    dense_grad = lax.all_gather(output_grad, "row", axis=1, tiled=True)[0]
    attn_grad = lax.psum_scatter(
        lax.dot_general(
            dense_grad, out_weight, (((1,), (1,)), ((), ())), preferred_element_type=jnp.float32
        ),
        "col",
        scatter_dimension=0,
        tiled=True,
    ).astype(jnp.bfloat16)
    grad_heads = attn_grad.reshape(local_rows, head_count, DH)
    prob_grad = jnp.einsum(
        "qhd,khd->hqk", grad_heads, all_values, preferred_element_type=jnp.float32
    )
    row_dot = jnp.transpose(
        jnp.sum(grad_heads.astype(jnp.float32) * attn_out.astype(jnp.float32), axis=2)
    )[:, :, None]
    score_grad = (attn_probs.astype(jnp.float32) * (prob_grad - row_dot)).astype(jnp.bfloat16)
    query_grad = (
        jnp.einsum("hqk,khd->qhd", score_grad, all_keys, preferred_element_type=jnp.float32)
        * factor
    )
    every_out = lax.all_gather(out_local, "col", axis=1, tiled=True)
    key_term = (
        jnp.einsum("hqk,qhd->khd", score_grad, local_query, preferred_element_type=jnp.float32)
        * factor
    )
    value_term = jnp.einsum(
        "hqk,qhd->khd", attn_probs, grad_heads, preferred_element_type=jnp.float32
    )
    key_sum, value_sum = (
        lax.psum_scatter(
            key_term.reshape(-1, feature_width).astype(jnp.bfloat16),
            "col",
            scatter_dimension=0,
            tiled=True,
        ).astype(jnp.float32),
        lax.psum_scatter(
            value_term.reshape(-1, feature_width).astype(jnp.bfloat16),
            "col",
            scatter_dimension=0,
            tiled=True,
        ).astype(jnp.float32),
    )
    out_pair = jnp.concatenate([every_out, swap_dp(every_out)], axis=0)
    grad_pair = lax.all_gather(
        jnp.concatenate([output_grad, grad_other], axis=0), "row", axis=1, tiled=True
    )
    patch_pair = jnp.concatenate([every_patch, patch_other], axis=0)
    out_weight_grad = lax.dot_general(
        out_pair, grad_pair, (((0, 1), (0, 1)), ((), ())), preferred_element_type=jnp.float32
    )
    embed_weight_grad = lax.dot_general(
        patch_pair, grad_pair, (((0, 1), (0, 1)), ((), ())), preferred_element_type=jnp.float32
    )
    return (
        query_grad.reshape(1, local_rows, feature_width),
        key_sum.reshape(1, local_rows, feature_width),
        value_sum.reshape(1, local_rows, feature_width),
        out_weight_grad,
        embed_weight_grad,
    )


def solution(mesh):
    placed = (
        P("dp", "col", "row"),
        P("dp", "col", "row"),
        P("dp", "col", "row"),
        P("dp", "col", "row"),
        P("row", "col"),
        P("dp", "row", "col"),
    )
    return jax.shard_map(
        body,
        mesh=mesh,
        in_specs=placed,
        out_specs=(
            P("dp", "col", "row"),
            P("dp", "col", "row"),
            P("dp", "col", "row"),
            P("row", "col"),
            P("row", "col"),
        ),
        check_vma=False,
    )
```

profile of v0, /device:TPU:0, one launch (start us, length us, event | category | flops | bytes accessed | tf_op | source)
XLA Modules:
  0.0 366.7 jit_solution(11999108349264509849)
XLA Ops:
  7.9 1.9 copy.22
  9.9 30.9 %all-gather.8.cloned.1.call-done = bf16[1,512,3072]{2,1,0:T(8,128)(2,1)} async-done(((bf16[1,128,3072]{2,1,0:T(8,128)(2,1)}), bf16[1,512,3072]{2,1,0:T(8,128)(2,1)}) %all-gather.8.cloned.1.call-update) | async-done | bytes 3145744 | tf_op jit(solution)/shard_map/all_gather | solution.py:45
  40.8 10.6 %fusion.3 = f32[512,1536]{1,0:T(8,128)} fusion(bf16[1536,3072]{1,0:T(8,128)(2,1)} %param.10, bf16[1,512,3072]{2,1,0:T(8,128)(2,1)} %all-gather.8.cloned.1.call-done), kind=kOutput, calls=%fused_computation.5 | convolution fusion | flops 4831838208 | bytes 15728640 | tf_op jit(solution)/shard_map/dot_general | solution.py:47
  53.7 27.0 %all-gather.6.cloned.1.call-done = bf16[1,512,1536]{1,2,0:T(8,128)(2,1)} async-done(((bf16[1,128,1536]{1,2,0:T(8,128)(2,1)}), bf16[1,512,1536]{1,2,0:T(8,128)(2,1)}) %all-gather.6.cloned.1.call-update) | async-done | bytes 1572880 | tf_op jit(solution)/shard_map/all_gather | solution.py:27
  80.7 2.1 multiply_reduce_fusion
  84.4 57.7 %reduce-scatter.4.cloned.1.call-done = f32[128,1536]{1,0:T(8,128)} async-done(((f32[512,1536]{1,0:T(8,128)}), f32[128,1536]{1,0:T(8,128)}) %reduce-scatter.4.cloned.1.call-update) | async-done | bytes 786448 | tf_op jit(solution)/shard_map/reduce_scatter | solution.py:46
  143.5 38.4 %all-gather.10.cloned.1.call-done = bf16[1,512,1536]{1,2,0:T(8,128)(2,1)} async-done(((bf16[1,128,1536]{1,2,0:T(8,128)(2,1)}), bf16[1,512,1536]{1,2,0:T(8,128)(2,1)}) %all-gather.10.cloned.1.call-update) | async-done | bytes 1572880 | tf_op jit(solution)/shard_map/all_gather | solution.py:28
  181.9 2.7 multiply_reduce_fusion.1
  186.3 17.8 %collective-permute-done.1 = bf16[1,128,3072]{2,1,0:T(8,128)(2,1)S(1)} collective-permute-done((bf16[1,128,3072]{2,1,0:T(8,128)(2,1)S(1)}, bf16[1,128,3072]{2,1,0:T(8,128)(2,1)S(1)}, u32[]{:S(2)}, u32[]{:S(2)}) %collective-permute-start.1) | collective-permute-done | bytes 786464 | tf_op jit(solution)/shard_map/ppermute | solution.py:16
  205.4 2.0 multiply_convert_fusion.1
  207.5 2.7 multiply_convert_fusion
  210.2 2.6 copy.29
  212.8 1.7 convolution_convert_fusion
  214.5 2.6 copy.30
  217.2 14.4 %all_gather.24 = bf16[1,512,364]{1,2,0:T(8,128)(2,1)S(1)} all-gather(bf16[1,128,364]{1,2,0:T(8,128)(2,1)S(1)} %copy-done.5), channel_id=1, replica_groups=mesh['dp'=2,'row'=4,'col'=4] {'col'}, dimensions={1}, use_global_device_ids=true | all-gather | bytes 465920 | tf_op jit(solution)/shard_map/all_gather | solution.py:29
  233.6 9.8 %collective-permute-done.2 = bf16[1,512,364]{1,2,0:T(8,128)(2,1)} collective-permute-done((bf16[1,512,364]{1,2,0:T(8,128)(2,1)S(1)}, bf16[1,512,364]{1,2,0:T(8,128)(2,1)}, u32[]{:S(2)}, u32[]{:S(2)}) %collective-permute-start.2) | collective-permute-done | bytes 372768 | tf_op jit(solution)/shard_map/ppermute | solution.py:16
  243.3 23.4 %all-gather.14.cloned.1.call-done = bf16[2,512,3072]{2,1,0:T(8,128)(2,1)} async-done(((bf16[2,128,3072]{2,1,0:T(8,128)(2,1)}), bf16[2,512,3072]{2,1,0:T(8,128)(2,1)}) %all-gather.14.cloned.1.call-update) | async-done | bytes 6291472 | tf_op jit(solution)/shard_map/all_gather | solution.py:89
  266.8 7.5 %convolution_bitcast_fusion.1 = f32[364,3072]{1,0:T(8,128)} fusion(bf16[2,512,3072]{2,1,0:T(8,128)(2,1)} %all-gather.14.cloned.1.call-done, bf16[1,512,364]{1,2,0:T(8,128)(2,1)} %collective-permute-done.2, bf16[1,512,364]{1,2,0:T(8,128)(2,1)S(1)} %all_gather.24), kind=kOutput, calls=%fused_computation.1 | convolution fusion | flops 2290462720 | bytes 11509760 | tf_op jit(solution)/shard_map/dot_general | solution.py:96
  275.8 2.4 copy.31
  278.2 26.8 %reduce-scatter.6.cloned.1.call-done = bf16[128,1536]{1,0:T(8,128)(2,1)} async-done(((bf16[512,1536]{1,0:T(8,128)(2,1)}), bf16[128,1536]{1,0:T(8,128)(2,1)}) %reduce-scatter.6.cloned.1.call-update) | async-done | bytes 393232 | tf_op jit(solution)/shard_map/reduce_scatter | solution.py:75
  305.0 2.0 bitcast_convert_fusion.1
  306.9 34.6 %reduce-scatter.8.cloned.1.call-done = bf16[128,1536]{1,0:T(8,128)(2,1)} async-done(((bf16[512,1536]{1,0:T(8,128)(2,1)}), bf16[128,1536]{1,0:T(8,128)(2,1)}) %reduce-scatter.8.cloned.1.call-update) | async-done | bytes 393232 | tf_op jit(solution)/shard_map/reduce_scatter | solution.py:81
  341.6 2.0 bitcast_convert_fusion
  343.5 16.3 %convolution_bitcast_fusion = f32[1536,3072]{1,0:T(8,128)} fusion(bf16[2,512,3072]{2,1,0:T(8,128)(2,1)} %all-gather.14.cloned.1.call-done, bf16[1,512,1536]{1,2,0:T(8,128)(2,1)} %collective-permute-done, bf16[1,512,1536]{1,2,0:T(8,128)(2,1)S(1)} %copy-done.6), kind=kOutput, calls=%fused_computation | convolution fusion | flops 9665249280 | bytes 28311552 | tf_op jit(solution)/shard_map/dot_general | solution.py:93
  (44 shorter events, 12.5 us)
Async XLA Ops:
  7.2 33.7 %all-gather.8.cloned.1.call-start = ((), (), s32[]{:S(2)}) async-start(), calls=%async_computation.4 | async-start | bytes 3932160 | tf_op jit(solution)/shard_map/all_gather | solution.py:45
  7.9 72.8 %all-gather.6.cloned.1.call-start = ((), (), s32[]{:S(2)}) async-start(), calls=%async_computation.3 | async-start | bytes 1966080 | tf_op jit(solution)/shard_map/all_gather | solution.py:27
  9.9 132.2 %reduce-scatter.4.cloned.1.call-start = ((), (), s32[]{:S(2)}) async-start(), calls=%async_computation.5 | async-start | bytes 3932160 | tf_op jit(solution)/shard_map/reduce_scatter | solution.py:46
  51.4 1.0 copy-start.3
  51.4 2.0 copy-start.4
  51.4 130.4 %all-gather.10.cloned.1.call-start = ((), (), s32[]{:S(2)}) async-start(), calls=%async_computation.6 | async-start | bytes 1966080 | tf_op jit(solution)/shard_map/all_gather | solution.py:28
  53.4 179.4 %all-gather.12.cloned.1.call-start = ((), (), s32[]{:S(2)}) async-start(), calls=%async_computation.9 | async-start | bytes 1966080 | tf_op jit(solution)/shard_map/all_gather | solution.py:66
  53.6 30.2 %copy-start.1 = (bf16[1,128,1536]{1,2,0:T(8,128)(2,1)}, bf16[1,128,1536]{1,2,0:T(8,128)(2,1)S(1)}, u32[]{:S(2)}) copy-start(bf16[1,128,1536]{1,2,0:T(8,128)(2,1)S(1)} %copy.21) | copy-start | bytes 1179652
  84.4 100.3 %copy-start.2 = (bf16[1,128,3072]{2,1,0:T(8,128)(2,1)S(1)}, bf16[1,128,3072]{2,1,0:T(8,128)(2,1)}, u32[]{:S(2)}) copy-start(bf16[1,128,3072]{2,1,0:T(8,128)(2,1)} %param.11) | copy-start | bytes 2359300
  184.6 82.2 %all-gather.14.cloned.1.call-start = ((), (), s32[]{:S(2)}) async-start(), calls=%async_computation.10 | async-start | bytes 7864320 | tf_op jit(solution)/shard_map/all_gather | solution.py:89
  184.7 19.3 %collective-permute-start.1 = (bf16[1,128,3072]{2,1,0:T(8,128)(2,1)S(1)}, bf16[1,128,3072]{2,1,0:T(8,128)(2,1)S(1)}, u32[]{:S(2)}, u32[]{:S(2)}) collective-permute-start(bf16[1,128,3072]{2,1,0:T(8,128)(2,1)S(1)} %copy-done.2), channel_id=1, source_target_pairs={{0,16},{16,0},{1,17},{17,1},{2,18},{18,2},{3,19},{19,3},{4,20},{20... | collective-permute-start | bytes 2359304 | tf_op jit(solution)/shard_map/ppermute | solution.py:16
  205.4 99.6 %reduce-scatter.6.cloned.1.call-start = ((), (), s32[]{:S(2)}) async-start(), calls=%async_computation.7 | async-start | bytes 1966080 | tf_op jit(solution)/shard_map/reduce_scatter | solution.py:75
  212.8 128.8 %reduce-scatter.8.cloned.1.call-start = ((), (), s32[]{:S(2)}) async-start(), calls=%async_computation.8 | async-start | bytes 1966080 | tf_op jit(solution)/shard_map/reduce_scatter | solution.py:81
  214.5 2.6 copy-start.5
  231.5 42.8 %copy-start = (bf16[1,512,1536]{1,2,0:T(8,128)(2,1)S(1)}, bf16[1,512,1536]{1,2,0:T(8,128)(2,1)}, u32[]{:S(2)}) copy-start(bf16[1,512,1536]{1,2,0:T(8,128)(2,1)} %all-gather.6.cloned.1.call-done) | copy-start | bytes 4718596
  231.5 11.8 %collective-permute-start.2 = (bf16[1,512,364]{1,2,0:T(8,128)(2,1)S(1)}, bf16[1,512,364]{1,2,0:T(8,128)(2,1)}, u32[]{:S(2)}, u32[]{:S(2)}) collective-permute-start(bf16[1,512,364]{1,2,0:T(8,128)(2,1)S(1)} %all_gather.24), channel_id=1, source_target_pairs={{0,16},{16,0},{1,17},{17,1},{2,18},{18,2},{3,19},{19,3},{4,20},{20... | collective-permute-start | bytes 1118216 | tf_op jit(solution)/shard_map/ppermute | solution.py:16
  232.7 110.8 %collective-permute-start = (bf16[1,512,1536]{1,2,0:T(8,128)(2,1)}, bf16[1,512,1536]{1,2,0:T(8,128)(2,1)}, u32[]{:S(2)}, u32[]{:S(2)}) collective-permute-start(bf16[1,512,1536]{1,2,0:T(8,128)(2,1)} %all-gather.12.cloned.1.call-done), channel_id=1, source_target_pairs={{0,16},{16,0},{1,17},{17,1},{2,18},{18,2},{3,19},{19,3},{4,20},{20... | collective-permute-start | bytes 4718600 | tf_op jit(solution)/shard_map/ppermute | solution.py:16
  275.8 67.8 %copy-start.6 = (bf16[1,512,1536]{1,2,0:T(8,128)(2,1)S(1)}, bf16[1,512,1536]{1,2,0:T(8,128)(2,1)}, u32[]{:S(2)}) copy-start(bf16[1,512,1536]{1,2,0:T(8,128)(2,1)} %all-gather.12.cloned.1.call-done) | copy-start | bytes 4718596
Sparse Core Ops, SparseCore 0:
  9.6 31.2 all-gather.7
  43.0 37.7 all-gather.5
  83.6 58.4 reduce-scatter.3
  144.1 37.7 all-gather.9
  184.7 35.9 all-gather.11
  222.1 44.5 all-gather.13
  269.6 35.3 reduce-scatter.5
  307.3 34.2 reduce-scatter.7
where the time goes:
time: 367 us
  waiting for transfers between devices  267 us (73%)
  matrix products  47.1 us (13%)
  blocking collectives  14.4 us (4%)
  between operations  14.2 us (4%)
  local copies, waits for them, and re-layouts  11.8 us (3%)
  other arithmetic  7.92 us (2%)
  starting transfers between devices  3.94 us (1%)
    reduce_scatter x1, waiting for transfers between devices, body(): lax.psum_scatter(lax.dot_general(dense_grad, out_weight, (((1,), (1,)), (...  57.7 us
    all_gather x1, waiting for transfers between devices, body(): lax.all_gather(attn_values, 'col', axis=1, tiled=True)  38.4 us
    reduce_scatter x1, waiting for transfers between devices, body(): lax.psum_scatter(value_term.reshape(-1, feature_width).astype(jnp.bfloat1...  34.6 us
    all_gather x1, waiting for transfers between devices, body(): dense_grad = lax.all_gather(output_grad, 'row', axis=1, tiled=True)[0]  30.9 us
    ppermute x3, waiting for transfers between devices, swap_dp(): return lax.ppermute(x, 'dp', [(0, 1), (1, 0)])  27.5 us
    all_gather x1, waiting for transfers between devices, body(): lax.all_gather(attn_keys, 'col', axis=1, tiled=True)  27 us
    reduce_scatter x1, waiting for transfers between devices, body(): lax.psum_scatter(key_term.reshape(-1, feature_width).astype(jnp.bfloat16)...  26.8 us
    all_gather x1, waiting for transfers between devices, body(): lax.all_gather(jnp.concatenate([output_grad, grad_other], axis=0), 'row',...  23.4 us
  transfers between devices with their start and end apart: 11, of which 9 were waited for; matrix products, arithmetic and copies ran while one was open for 13% of the time, Pallas kernels for 0%

commit v1 on v0

--- a/solution.py
+++ b/solution.py
@@ -4,6 +4,29 @@
 from jax.sharding import PartitionSpec as P
 
 DH = 128
+
+
+def bind_teams(original):
+    vec_out, m_next, reached = (lax.axis_size("col"), lax.axis_index("col"), original.shape[1])
+    shelf = [(dev_j, (dev_j + 1) % vec_out) for dev_j in range(vec_out)]
+    row_list = [(dev_j, (dev_j - 1) % vec_out) for dev_j in range(vec_out)]
+    back = jnp.zeros((*original.shape[:1], vec_out * reached, *original.shape[2:]), original.dtype)
+    back = lax.dynamic_update_slice_in_dim(back, original, m_next * reached, axis=1)
+    spare = carry = original
+    f_now = vec_out // 2
+    i0 = 1
+    while i0 < f_now + 1:
+        spare = lax.ppermute(spare, axis_name="col", perm=shelf)
+        back = lax.dynamic_update_slice_in_dim(
+            back, spare, (m_next - i0) % vec_out * reached, axis=1
+        )
+        if i0 < vec_out - f_now:
+            carry = lax.ppermute(carry, "col", row_list)
+            back = lax.dynamic_update_slice_in_dim(
+                back, carry, (m_next + i0) % vec_out * reached, axis=1
+            )
+        i0 += 1
+    return back
 
 
 def contract_rows(left, right):
@@ -25,7 +48,7 @@
     patch_other = swap_dp(lax.all_gather(patches, "col", axis=1, tiled=True))
     every_key, every_value, every_patch = (
         lax.all_gather(attn_keys, "col", axis=1, tiled=True),
-        lax.all_gather(attn_values, "col", axis=1, tiled=True),
+        bind_teams(attn_values),
         lax.all_gather(patches, "col", axis=1, tiled=True),
     )
     local_query = queries[0].reshape(local_rows, head_count, DH)

time: 367 us -> 355 us (0.967)
  waiting for transfers between devices: 267 us -> 237 us
  starting transfers between devices: 3.94 us -> 17.2 us
  local copies, waits for them, and re-layouts: 11.8 us -> 16.1 us
    all_gather x1 -> x0, waiting for transfers between devices: 38.4 us -> none  [body(): lax.all_gather(attn_values, 'col', axis=1, tiled=True)]
    ppermute x0 -> x3, waiting for transfers between devices: none -> 37.6 us  [the longest x2 31.7 us: bind_teams(): spare = lax.ppermute(spare, axis_name='col', perm=shelf)]
    all_gather x1, waiting for transfers between devices: 27 us -> 0.02 us  [body(): lax.all_gather(attn_keys, 'col', axis=1, tiled=True)]
    ppermute x0 -> x3, starting transfers between devices: none -> 13.4 us  [the longest x2 11.1 us: bind_teams(): spare = lax.ppermute(spare, axis_name='col', perm=shelf)]
  transfers between devices with their start and end apart: 11 -> 13, of which waited for: 9 -> 10; matrix products, arithmetic and copies ran while one was open for 13% -> 14% of each run, Pallas kernels for 0% -> 0%
where the time goes in v1:
time: 355 us
  waiting for transfers between devices  237 us (67%)
  matrix products  45.3 us (13%)
  starting transfers between devices  17.2 us (5%)
  local copies, waits for them, and re-layouts  16.1 us (5%)
  blocking collectives  14.5 us (4%)
  between operations  14.4 us (4%)
  other arithmetic  9.82 us (3%)
    reduce_scatter x1, waiting for transfers between devices, body(): lax.psum_scatter(lax.dot_general(dense_grad, out_weight, (((1,), (1,)), (...  55 us
    reduce_scatter x1, waiting for transfers between devices, body(): lax.psum_scatter(value_term.reshape(-1, feature_width).astype(jnp.bfloat1...  34.7 us
    ppermute x2, waiting for transfers between devices, bind_teams(): spare = lax.ppermute(spare, axis_name='col', perm=shelf)  31.7 us
    all_gather x1, waiting for transfers between devices, body(): dense_grad = lax.all_gather(output_grad, 'row', axis=1, tiled=True)[0]  30.9 us
    ppermute x3, waiting for transfers between devices, swap_dp(): return lax.ppermute(x, 'dp', [(0, 1), (1, 0)])  27.6 us
    reduce_scatter x1, waiting for transfers between devices, body(): lax.psum_scatter(key_term.reshape(-1, feature_width).astype(jnp.bfloat16)...  26.6 us
    all_gather x1, waiting for transfers between devices, body(): lax.all_gather(jnp.concatenate([output_grad, grad_other], axis=0), 'row',...  24 us
    dot_general x1, matrix products, body(): lax.dot_general(out_pair, grad_pair, (((0, 1), (0, 1)), ((), ())), prefer...  16.3 us
  transfers between devices with their start and end apart: 13, of which 10 were waited for; matrix products, arithmetic and copies ran while one was open for 14% of the time, Pallas kernels for 0%

profile of v1, /device:TPU:0, one launch (start us, length us, event | category | flops | bytes accessed | tf_op | source)
XLA Modules:
  0.0 354.6 jit_solution(14212232972553949455)
XLA Ops:
  9.9 30.9 %all-gather.7.cloned.1.call-done = bf16[1,512,3072]{2,1,0:T(8,128)(2,1)} async-done(((bf16[1,128,3072]{2,1,0:T(8,128)(2,1)}), bf16[1,512,3072]{2,1,0:T(8,128)(2,1)}) %all-gather.7.cloned.1.call-update) | async-done | bytes 3145744 | tf_op jit(solution)/shard_map/all_gather | solution.py:68
  40.8 10.6 %fusion.3 = f32[512,1536]{1,0:T(8,128)} fusion(bf16[1536,3072]{1,0:T(8,128)(2,1)} %param.10, bf16[1,512,3072]{2,1,0:T(8,128)(2,1)} %all-gather.7.cloned.1.call-done), kind=kOutput, calls=%fused_computation.5 | convolution fusion | flops 4831838208 | bytes 15728640 | tf_op jit(solution)/shard_map/dot_general | solution.py:70
  53.9 2.3 collective-permute-start.1
  57.0 17.6 %collective-permute-done = bf16[1,128,1536]{2,1,0:T(8,128)(2,1)S(1)} collective-permute-done((bf16[1,128,1536]{2,1,0:T(8,128)(2,1)S(1)}, bf16[1,128,1536]{2,1,0:T(8,128)(2,1)S(1)}, u32[]{:S(2)}, u32[]{:S(2)}) %collective-permute-start) | collective-permute-done | bytes 393248 | tf_op jit(solution)/shard_map/ppermute | solution.py:19
  74.8 9.6 %collective-permute-start.2 = (bf16[1,128,1536]{2,1,0:T(8,128)(2,1)S(1)}, bf16[1,128,1536]{2,1,0:T(8,128)(2,1)}, u32[]{:S(2)}, u32[]{:S(2)}) collective-permute-start(bf16[1,128,1536]{2,1,0:T(8,128)(2,1)S(1)} %collective-permute-done), channel_id=1, source_target_pairs={{0,1},{1,2},{2,3},{3,0},{4,5},{5,6},{6,7},{7,4},{8,9},{9,10},{10,1... | collective-permute-start | bytes 1179656 | tf_op jit(solution)/shard_map/ppermute | solution.py:19
  84.4 5.9 %collective-permute-done.1 = bf16[1,128,1536]{2,1,0:T(8,128)(2,1)} collective-permute-done((bf16[1,128,1536]{2,1,0:T(8,128)(2,1)S(1)}, bf16[1,128,1536]{2,1,0:T(8,128)(2,1)}, u32[]{:S(2)}, u32[]{:S(2)}) %collective-permute-start.1) | collective-permute-done | bytes 393248 | tf_op jit(solution)/shard_map/ppermute | solution.py:24
  91.7 14.1 %collective-permute-done.2 = bf16[1,128,1536]{2,1,0:T(8,128)(2,1)} collective-permute-done((bf16[1,128,1536]{2,1,0:T(8,128)(2,1)S(1)}, bf16[1,128,1536]{2,1,0:T(8,128)(2,1)}, u32[]{:S(2)}, u32[]{:S(2)}) %collective-permute-start.2) | collective-permute-done | bytes 393248 | tf_op jit(solution)/shard_map/ppermute | solution.py:19
  107.2 2.6 multiply_reduce_fusion
  111.4 55.0 %reduce-scatter.4.cloned.1.call-done = f32[128,1536]{1,0:T(8,128)} async-done(((f32[512,1536]{1,0:T(8,128)}), f32[128,1536]{1,0:T(8,128)}) %reduce-scatter.4.cloned.1.call-update) | async-done | bytes 786448 | tf_op jit(solution)/shard_map/reduce_scatter | solution.py:69
  172.5 17.9 %collective-permute-done.4 = bf16[1,128,3072]{2,1,0:T(8,128)(2,1)S(1)} collective-permute-done((bf16[1,128,3072]{2,1,0:T(8,128)(2,1)}, bf16[1,128,3072]{2,1,0:T(8,128)(2,1)S(1)}, u32[]{:S(2)}, u32[]{:S(2)}) %collective-permute-start.4) | collective-permute-done | bytes 786464 | tf_op jit(solution)/shard_map/ppermute | solution.py:39
  190.3 2.5 pad_maximum_fusion
  192.9 2.1 multiply_convert_fusion.1
  196.7 2.6 copy.36
  201.1 2.6 copy.37
  204.6 14.5 %all_gather.20 = bf16[1,512,364]{1,2,0:T(8,128)(2,1)S(1)} all-gather(bf16[1,128,364]{1,2,0:T(8,128)(2,1)S(1)} %copy-done.6), channel_id=1, replica_groups=mesh['dp'=2,'row'=4,'col'=4] {'col'}, dimensions={1}, use_global_device_ids=true | all-gather | bytes 465920 | tf_op jit(solution)/shard_map/all_gather | solution.py:52
  221.1 9.8 %collective-permute-done.5 = bf16[1,512,364]{1,2,0:T(8,128)(2,1)} collective-permute-done((bf16[1,512,364]{1,2,0:T(8,128)(2,1)S(1)}, bf16[1,512,364]{1,2,0:T(8,128)(2,1)}, u32[]{:S(2)}, u32[]{:S(2)}) %collective-permute-start.5) | collective-permute-done | bytes 372768 | tf_op jit(solution)/shard_map/ppermute | solution.py:39
  230.9 24.0 %all-gather.11.cloned.1.call-done = bf16[2,512,3072]{2,1,0:T(8,128)(2,1)} async-done(((bf16[2,128,3072]{2,1,0:T(8,128)(2,1)}), bf16[2,512,3072]{2,1,0:T(8,128)(2,1)}) %all-gather.11.cloned.1.call-update) | async-done | bytes 6291472 | tf_op jit(solution)/shard_map/all_gather | solution.py:112
  254.8 7.5 %convolution_bitcast_fusion.1 = f32[364,3072]{1,0:T(8,128)} fusion(bf16[2,512,3072]{2,1,0:T(8,128)(2,1)} %all-gather.11.cloned.1.call-done, bf16[1,512,364]{1,2,0:T(8,128)(2,1)} %collective-permute-done.5, bf16[1,512,364]{1,2,0:T(8,128)(2,1)S(1)} %all_gather.20), kind=kOutput, calls=%fused_computation.1 | convolution fusion | flops 2290462720 | bytes 11509760 | tf_op jit(solution)/shard_map/dot_general | solution.py:119
  263.8 2.4 copy.38
  266.2 26.6 %reduce-scatter.6.cloned.1.call-done = bf16[128,1536]{1,0:T(8,128)(2,1)} async-done(((bf16[512,1536]{1,0:T(8,128)(2,1)}), bf16[128,1536]{1,0:T(8,128)(2,1)}) %reduce-scatter.6.cloned.1.call-update) | async-done | bytes 393232 | tf_op jit(solution)/shard_map/reduce_scatter | solution.py:98
  292.9 2.0 bitcast_convert_fusion.1
  294.8 34.7 %reduce-scatter.8.cloned.1.call-done = bf16[128,1536]{1,0:T(8,128)(2,1)} async-done(((bf16[512,1536]{1,0:T(8,128)(2,1)}), bf16[128,1536]{1,0:T(8,128)(2,1)}) %reduce-scatter.8.cloned.1.call-update) | async-done | bytes 393232 | tf_op jit(solution)/shard_map/reduce_scatter | solution.py:104
  329.5 2.0 bitcast_convert_fusion
  331.5 16.3 %convolution_bitcast_fusion = f32[1536,3072]{1,0:T(8,128)} fusion(bf16[2,512,3072]{2,1,0:T(8,128)(2,1)} %all-gather.11.cloned.1.call-done, bf16[1,512,1536]{1,2,0:T(8,128)(2,1)} %collective-permute-done.3, bf16[1,512,1536]{1,2,0:T(8,128)(2,1)S(1)} %copy-done.7), kind=kOutput, calls=%fused_computation | convolution fusion | flops 9665249280 | bytes 28311552 | tf_op jit(solution)/shard_map/dot_general | solution.py:116
  (57 shorter events, 24.3 us)
Async XLA Ops:
  7.2 33.7 %all-gather.7.cloned.1.call-start = ((), (), s32[]{:S(2)}) async-start(), calls=%async_computation.4 | async-start | bytes 3932160 | tf_op jit(solution)/shard_map/all_gather | solution.py:68
  7.9 99.3 %all-gather.5.cloned.1.call-start = ((), (), s32[]{:S(2)}) async-start(), calls=%async_computation.3 | async-start | bytes 1966080 | tf_op jit(solution)/shard_map/all_gather | solution.py:50
  9.9 156.5 %reduce-scatter.4.cloned.1.call-start = ((), (), s32[]{:S(2)}) async-start(), calls=%async_computation.5 | async-start | bytes 3932160 | tf_op jit(solution)/shard_map/reduce_scatter | solution.py:69
  51.4 1.0 copy-start.5
  51.4 5.1 %copy-start.4 = (bf16[1,128,1536]{2,1,0:T(8,128)(2,1)S(1)}, bf16[1,128,1536]{2,1,0:T(8,128)(2,1)}, u32[]{:S(2)}) copy-start(bf16[1,128,1536]{2,1,0:T(8,128)(2,1)} %param.7) | copy-start | bytes 1179652
  51.4 169.2 %all-gather.9.cloned.1.call-start = ((), (), s32[]{:S(2)}) async-start(), calls=%async_computation.8 | async-start | bytes 1966080 | tf_op jit(solution)/shard_map/all_gather | solution.py:89
  52.4 22.2 %collective-permute-start = (bf16[1,128,1536]{2,1,0:T(8,128)(2,1)S(1)}, bf16[1,128,1536]{2,1,0:T(8,128)(2,1)S(1)}, u32[]{:S(2)}, u32[]{:S(2)}) collective-permute-start(bf16[1,128,1536]{2,1,0:T(8,128)(2,1)S(1)} %copy-done.5), channel_id=1, source_target_pairs={{0,1},{1,2},{2,3},{3,0},{4,5},{5,6},{6,7},{7,4},{8,9},{9,10},{10,1... | collective-permute-start | bytes 1179656 | tf_op jit(solution)/shard_map/ppermute | solution.py:19
  53.9 36.4 %collective-permute-start.1 = (bf16[1,128,1536]{2,1,0:T(8,128)(2,1)S(1)}, bf16[1,128,1536]{2,1,0:T(8,128)(2,1)}, u32[]{:S(2)}, u32[]{:S(2)}) collective-permute-start(bf16[1,128,1536]{2,1,0:T(8,128)(2,1)S(1)} %copy-done.5), channel_id=1, source_target_pairs={{0,3},{1,0},{2,1},{3,2},{4,7},{5,4},{6,5},{7,6},{8,11},{9,8},{10,9... | collective-permute-start | bytes 1179656 | tf_op jit(solution)/shard_map/ppermute | solution.py:24
  56.8 50.5 %copy-start.2 = (bf16[1,128,1536]{1,2,0:T(8,128)(2,1)}, bf16[1,128,1536]{1,2,0:T(8,128)(2,1)S(1)}, u32[]{:S(2)}) copy-start(bf16[1,128,1536]{1,2,0:T(8,128)(2,1)S(1)} %copy.25) | copy-start | bytes 1179652
  74.8 31.0 %collective-permute-start.2 = (bf16[1,128,1536]{2,1,0:T(8,128)(2,1)S(1)}, bf16[1,128,1536]{2,1,0:T(8,128)(2,1)}, u32[]{:S(2)}, u32[]{:S(2)}) collective-permute-start(bf16[1,128,1536]{2,1,0:T(8,128)(2,1)S(1)} %collective-permute-done), channel_id=1, source_target_pairs={{0,1},{1,2},{2,3},{3,0},{4,5},{5,6},{6,7},{7,4},{8,9},{9,10},{10,1... | collective-permute-start | bytes 1179656 | tf_op jit(solution)/shard_map/ppermute | solution.py:19
  107.2 62.4 %copy-start = (bf16[1,512,1536]{1,2,0:T(8,128)(2,1)}, bf16[1,512,1536]{1,2,0:T(8,128)(2,1)S(1)}, u32[]{:S(2)}) copy-start(bf16[1,512,1536]{1,2,0:T(8,128)(2,1)S(1)} %constant_dynamic-update-slice_fusion) | copy-start | bytes 4718596
  170.9 83.9 %all-gather.11.cloned.1.call-start = ((), (), s32[]{:S(2)}) async-start(), calls=%async_computation.9 | async-start | bytes 7864320 | tf_op jit(solution)/shard_map/all_gather | solution.py:112
  171.0 19.4 %collective-permute-start.4 = (bf16[1,128,3072]{2,1,0:T(8,128)(2,1)}, bf16[1,128,3072]{2,1,0:T(8,128)(2,1)S(1)}, u32[]{:S(2)}, u32[]{:S(2)}) collective-permute-start(bf16[1,128,3072]{2,1,0:T(8,128)(2,1)} %param.11), channel_id=1, source_target_pairs={{0,16},{16,0},{1,17},{17,1},{2,18},{18,2},{3,19},{19,3},{4,20},{20... | collective-permute-start | bytes 2359304 | tf_op jit(solution)/shard_map/ppermute | solution.py:39
  192.8 100.0 %reduce-scatter.6.cloned.1.call-start = ((), (), s32[]{:S(2)}) async-start(), calls=%async_computation.6 | async-start | bytes 1966080 | tf_op jit(solution)/shard_map/reduce_scatter | solution.py:98
  192.9 2.1 copy-start.3
  199.3 130.2 %reduce-scatter.8.cloned.1.call-start = ((), (), s32[]{:S(2)}) async-start(), calls=%async_computation.7 | async-start | bytes 1966080 | tf_op jit(solution)/shard_map/reduce_scatter | solution.py:104
  203.7 0.9 copy-start.6
  219.1 43.3 %copy-start.1 = (bf16[1,512,1536]{1,2,0:T(8,128)(2,1)S(1)}, bf16[1,512,1536]{1,2,0:T(8,128)(2,1)}, u32[]{:S(2)}) copy-start(bf16[1,512,1536]{1,2,0:T(8,128)(2,1)} %all-gather.5.cloned.1.call-done) | copy-start | bytes 4718596
  219.1 11.8 %collective-permute-start.5 = (bf16[1,512,364]{1,2,0:T(8,128)(2,1)S(1)}, bf16[1,512,364]{1,2,0:T(8,128)(2,1)}, u32[]{:S(2)}, u32[]{:S(2)}) collective-permute-start(bf16[1,512,364]{1,2,0:T(8,128)(2,1)S(1)} %all_gather.20), channel_id=1, source_target_pairs={{0,16},{16,0},{1,17},{17,1},{2,18},{18,2},{3,19},{19,3},{4,20},{20... | collective-permute-start | bytes 1118216 | tf_op jit(solution)/shard_map/ppermute | solution.py:39
  220.6 110.8 %collective-permute-start.3 = (bf16[1,512,1536]{1,2,0:T(8,128)(2,1)}, bf16[1,512,1536]{1,2,0:T(8,128)(2,1)}, u32[]{:S(2)}, u32[]{:S(2)}) collective-permute-start(bf16[1,512,1536]{1,2,0:T(8,128)(2,1)} %all-gather.9.cloned.1.call-done), channel_id=1, source_target_pairs={{0,16},{16,0},{1,17},{17,1},{2,18},{18,2},{3,19},{19,3},{4,20},{20... | collective-permute-start | bytes 4718600 | tf_op jit(solution)/shard_map/ppermute | solution.py:39
  263.8 67.6 %copy-start.7 = (bf16[1,512,1536]{1,2,0:T(8,128)(2,1)S(1)}, bf16[1,512,1536]{1,2,0:T(8,128)(2,1)}, u32[]{:S(2)}) copy-start(bf16[1,512,1536]{1,2,0:T(8,128)(2,1)} %all-gather.9.cloned.1.call-done) | copy-start | bytes 4718596
Sparse Core Ops, SparseCore 0:
  9.6 31.2 all-gather.6
  43.0 58.8 all-gather.4
  104.7 61.6 reduce-scatter.3
  171.0 37.7 all-gather.8
  210.2 44.5 all-gather.10
  257.6 35.2 reduce-scatter.5
  295.2 34.2 reduce-scatter.7
